TPU v7x, 32 devices: a whole 2x2x4 slice. The times are simulated.
32 devices in a mesh: segment: 2 (over core), expert: 16 (over z, y, x).
Axes of the slice: x: 2, y: 2, z: 4, core: 2. Of those that a mesh axis runs over, the one named last changes fastest.
Arguments:
- hidden_in: bfloat16 [2, 256, 7168], P('segment', 'expert'), may hold values from -6 to 6
- norm_gain: bfloat16 [2, 7168], P('segment'), may hold values from 0.25 to 1.75
- up_proj: bfloat16 [2, 8192, 7168], P('segment', 'expert'), may hold values from -0.0625 to 0.0625
- down_proj: bfloat16 [2, 8192, 7168], P('segment', 'expert'), may hold values from -0.1875 to 0.1875
- expert_ids: int32 [2, 256, 2], P('segment', 'expert'), may hold values from 0 to 7, all different within a row; in each aligned block of 16 rows (0 to 15, 16 to 31, ..., all dimensions but the last counted through in order) at most 7 rows name the same one
- gate_weights: float32 [2, 256, 2], P('segment', 'expert'), may hold values from 0.2 to 1
Outputs:
- handed_on: bfloat16 [2, 256, 7168], P('segment', 'expert')
Inputs may be any that keep to these rules, and one draw needn't show every extreme that they name: `expert_ids`: each row names 2 different experts. Among the rows of one device in one section no expert is named by more than 7 rows, and in some device an expert is named by exactly 7.
All inputs are finite; a program needn't handle non-finite values.
Results may differ from a plain program's by a relative error of at most 0.0075.
Values may be sent and summed in bfloat16 or wider, within the bound.
No kernel may reach another device: no remote copies, remote signals or barrier semaphores. Data moves between devices by JAX's collectives and lax.ppermute only.
A program may use at most 64 MiB of HBM per device.

v0:
```python
import jax
import jax.numpy as jnp
from jax import lax
from jax.sharding import PartitionSpec as P

EXPERTS = 8
CAP = 7
SLOTS = 8


def passed_along(shard, axis, by):
    count = lax.axis_size(axis)
    return lax.ppermute(shard, axis, [(i, (i + by) % count) for i in range(count)])


def shards(hidden_in, norm_gain, up_proj, down_proj, expert_ids, gate_weights):
    members = lax.axis_size("expert")
    per_group = members // EXPERTS
    tokens = hidden_in[0]
    gain = norm_gain[0]
    up_block = up_proj[0]
    down_block = down_proj[0]
    routes = expert_ids[0]
    weights = gate_weights[0]
    rows_here, width = tokens.shape
    top = routes.shape[1]
    stacked, chosen = lax.optimization_barrier(
        (
            jnp.concatenate([tokens, gain[None, :]], axis=0).astype(jnp.float32),
            (routes[:, :, None] == jnp.arange(EXPERTS)[None, None, :]).astype(jnp.int32),
        )
    )
    wide = stacked[:rows_here]
    square = jnp.mean(wide**2, axis=-1, keepdims=True)
    normed = (wide * lax.rsqrt(square + 1e-06) * stacked[rows_here:]).astype(jnp.bfloat16)
    named = jnp.sum(chosen, axis=1)
    positions = jnp.arange(rows_here)
    earlier = (positions[None, :] < positions[:, None]).astype(jnp.int32)
    before = jnp.dot(earlier, named, preferred_element_type=jnp.int32)
    places = jnp.arange(EXPERTS)[None, None, :] * SLOTS + before[:, None, :]
    key = jnp.sum(chosen * places, axis=2)
    slot = jnp.arange(members * SLOTS)
    slot_device = slot % members
    slot_rank = slot // members
    slot_expert = slot_device // per_group
    hits = key[None, :, :] == (slot_expert * SLOTS + slot_rank)[:, None, None]
    picker = jnp.any(hits, axis=2).astype(jnp.bfloat16)
    outgoing = jnp.dot(picker, normed, preferred_element_type=jnp.float32).astype(jnp.bfloat16)
    outgoing = outgoing.reshape(SLOTS, members, width)
    incoming = lax.all_to_all(outgoing, "expert", split_axis=1, concat_axis=1, tiled=True)
    inner = jnp.einsum("psd,fd->psf", incoming, up_block, preferred_element_type=jnp.float32)
    active = jax.nn.silu(inner).astype(jnp.bfloat16)
    active = lax.optimization_barrier(active.transpose(1, 0, 2).reshape(members * SLOTS, -1))
    partial = jnp.dot(active, down_block, preferred_element_type=jnp.float32).astype(jnp.bfloat16)
    partial = partial.reshape(members, SLOTS, width)
    returned = lax.all_to_all(partial, "expert", split_axis=0, concat_axis=0, tiled=True).transpose(
        1, 0, 2
    )
    combine = jnp.sum(jnp.where(hits, weights[None, :, :], 0.0), axis=2).T.reshape(
        rows_here, SLOTS, members
    )
    combine_hi = combine.astype(jnp.bfloat16)
    combine_lo = (combine - combine_hi.astype(jnp.float32)).astype(jnp.bfloat16)
    mixture = jnp.einsum("rps,psd->rd", combine_hi, returned, preferred_element_type=jnp.float32)
    mixture = mixture + jnp.einsum(
        "rps,psd->rd", combine_lo, returned, preferred_element_type=jnp.float32
    )
    section_out = (tokens.astype(jnp.float32) + mixture).astype(jnp.bfloat16)
    handed = passed_along(section_out, "segment", 1)
    return handed[None]


def solution(mesh):
    in_specs = (
        P("segment", "expert", None),
        P("segment", None),
        P("segment", "expert", None),
        P("segment", "expert", None),
        P("segment", "expert", None),
        P("segment", "expert", None),
    )
    out_specs = P("segment", "expert", None)
    return jax.shard_map(shards, mesh=mesh, in_specs=in_specs, out_specs=out_specs, check_vma=False)
```

profile of v0, /device:TPU:13, one launch (start us, length us, event | category | flops | bytes accessed | tf_op | source)
XLA Modules:
  0.0 109.0 jit_solution(2199640007725550292)
XLA Ops:
  0.0 0.7 fusion.20
  0.7 1.0 maximum_convert_fusion
  1.7 0.2 multiply_reduce_fusion
  1.9 0.1 convolution_add_fusion
  2.0 0.1 multiply_reduce_fusion.1
  2.1 0.1 compare_reduce_fusion
  2.2 0.7 convolution_convert_fusion.1
  2.8 1.0 copy.30
  3.9 0.0 slice-start
  3.9 48.2 %all_to_all.10 = bf16[8,16,7168]{2,0,1:T(8,128)(2,1)S(1)} all-to-all(bf16[8,16,7168]{2,0,1:T(8,128)(2,1)S(1)} %copy.30), channel_id=1, replica_groups=mesh['segment'=2,'expert'=16] {'expert'}, dimensions={1} | all-to-all | bytes 3670016 | tf_op jit(solution)/shard_map/all_to_all | solution.py:50
  52.0 0.0 copy-done
  52.1 2.5 %fusion.14 = bf16[128,512]{1,0:T(8,128)(2,1)S(1)} fusion(bf16[8,16,7168]{2,0,1:T(8,128)(2,1)S(1)} %all_to_all.10, bf16[1,512,7168]{2,1,0:T(8,128)(2,1)S(1)} %copy-done), kind=kOutput, calls=%fused_computation.19 | convolution fusion | flops 939851776 | bytes 9306112 | tf_op jit(solution)/shard_map/psd,fd->psf/dot_general | solution.py:51
  54.6 2.4 %fusion = bf16[16,8,7168]{2,1,0:T(8,128)(2,1)} fusion(bf16[128,512]{1,0:T(8,128)(2,1)S(1)} %fusion.14, bf16[1,512,7168]{2,1,0:T(8,128)(2,1)S(1)} %bitcast.53), kind=kOutput, calls=%fused_computation.2 | convolution fusion | flops 940441600 | bytes 9306112 | tf_op jit(solution)/shard_map/dot_general | solution.py:54
  57.0 5.2 %all-to-all-start.1 = ((bf16[16,8,7168]{2,1,0:T(8,128)(2,1)}), bf16[16,8,7168]{2,1,0:T(8,128)(2,1)S(1)}, u32[]{:S(2)}, u32[]{:S(2)}) async-start(bf16[16,8,7168]{2,1,0:T(8,128)(2,1)} %fusion), calls=%async_computation.1 | async-start | bytes 3670016 | tf_op jit(solution)/shard_map/all_to_all | solution.py:56
  62.2 0.1 fusion.19
  62.3 0.1 reshape.68
  62.4 0.1 copy.32
  62.5 0.1 copy.31
  62.6 42.2 %all-to-all-done.1 = bf16[16,8,7168]{2,1,0:T(8,128)(2,1)S(1)} async-done(((bf16[16,8,7168]{2,1,0:T(8,128)(2,1)}), bf16[16,8,7168]{2,1,0:T(8,128)(2,1)S(1)}, u32[]{:S(2)}, u32[]{:S(2)}) %all-to-all-start.1) | async-done | bytes 1835040 | tf_op jit(solution)/shard_map/all_to_all | solution.py:56
  104.8 0.4 convolution_bitcast_fusion
  105.2 0.4 fusion.3
  105.7 1.5 %collective-permute-start = (bf16[16,7168]{1,0:T(8,128)(2,1)S(1)}, bf16[16,7168]{1,0:T(8,128)(2,1)S(1)}, u32[]{:S(2)}, u32[]{:S(2)}) collective-permute-start(bf16[16,7168]{1,0:T(8,128)(2,1)S(1)} %fusion.3), channel_id=1, source_target_pairs={{0,16},{16,0},{1,17},{17,1},{2,18},{18,2},{3,19},{19,3},{4,20},{20... | collective-permute-start | bytes 688136 | tf_op jit(solution)/shard_map/ppermute | solution.py:13
  107.2 1.1 %collective-permute-done = bf16[16,7168]{1,0:T(8,128)(2,1)S(1)} collective-permute-done((bf16[16,7168]{1,0:T(8,128)(2,1)S(1)}, bf16[16,7168]{1,0:T(8,128)(2,1)S(1)}, u32[]{:S(2)}, u32[]{:S(2)}) %collective-permute-start) | collective-permute-done | bytes 229408 | tf_op jit(solution)/shard_map/ppermute | solution.py:13
  108.3 0.7 copy.34
  (15 shorter events, 0.1 us)
Async XLA Ops:
  2.2 49.9 %copy-start = (bf16[1,512,7168]{2,1,0:T(8,128)(2,1)S(1)}, bf16[1,512,7168]{2,1,0:T(8,128)(2,1)}, u32[]{:S(2)}) copy-start(bf16[1,512,7168]{2,1,0:T(8,128)(2,1)} %param.8) | copy-start | bytes 22020100
  3.9 50.7 %slice-start = ((s8[7340032]{0:T(1024)(128)(4,1)}), s8[4194304]{0:T(1024)(128)(4,1)S(1)}, s32[]{:S(2)}) async-start(s8[7340032]{0:T(1024)(128)(4,1)} %bitcast.52), calls=%async_computation.2 | async-start | bytes 8388608
  52.0 2.6 %slice-start.1 = ((s8[7340032]{0:T(1024)(128)(4,1)}), s8[3145728]{0:T(1024)(128)(4,1)S(1)}, s32[]{:S(2)}) async-start(s8[7340032]{0:T(1024)(128)(4,1)} %bitcast.52), calls=%async_computation.3 | async-start | bytes 6291456
  57.0 5.2 %copy-start.2 = (f32[1,16,2]{1,2,0:T(2,128)S(1)}, f32[1,16,2]{1,2,0:T(2,128)}, u32[]{:S(2)}) copy-start(f32[1,16,2]{1,2,0:T(2,128)} %param.11) | copy-start | bytes 388
  57.0 47.8 %all-to-all-start.1 = ((bf16[16,8,7168]{2,1,0:T(8,128)(2,1)}), bf16[16,8,7168]{2,1,0:T(8,128)(2,1)S(1)}, u32[]{:S(2)}, u32[]{:S(2)}) async-start(bf16[16,8,7168]{2,1,0:T(8,128)(2,1)} %fusion), calls=%async_computation.1 | async-start | bytes 3670016 | tf_op jit(solution)/shard_map/all_to_all | solution.py:56
  62.2 43.0 %copy-start.1 = (bf16[1,16,7168]{2,1,0:T(8,128)(2,1)S(1)}, bf16[1,16,7168]{2,1,0:T(8,128)(2,1)}, u32[]{:S(2)}) copy-start(bf16[1,16,7168]{2,1,0:T(8,128)(2,1)} %param.6) | copy-start | bytes 688132
  105.7 2.6 %collective-permute-start = (bf16[16,7168]{1,0:T(8,128)(2,1)S(1)}, bf16[16,7168]{1,0:T(8,128)(2,1)S(1)}, u32[]{:S(2)}, u32[]{:S(2)}) collective-permute-start(bf16[16,7168]{1,0:T(8,128)(2,1)S(1)} %fusion.3), channel_id=1, source_target_pairs={{0,16},{16,0},{1,17},{17,1},{2,18},{18,2},{3,19},{19,3},{4,20},{20... | collective-permute-start | bytes 688136 | tf_op jit(solution)/shard_map/ppermute | solution.py:13
where the time goes:
time: 109 us
  blocking collectives  48.2 us (44%)
  waiting for transfers between devices  43.3 us (40%)
  starting transfers between devices  6.71 us (6%)
  matrix products  6.51 us (6%)
  other arithmetic  2.12 us (2%)
  local copies, waits for them, and re-layouts  2.05 us (2%)
    all_to_all x1, blocking collectives, shards(): lax.all_to_all(outgoing, 'expert', split_axis=1, concat_axis=1, tiled=True)  48.2 us
    all_to_all x1, waiting for transfers between devices, shards(): lax.all_to_all(partial, 'expert', split_axis=0, concat_axis=0, tiled=True)  42.2 us
    all_to_all x1, starting transfers between devices, shards(): lax.all_to_all(partial, 'expert', split_axis=0, concat_axis=0, tiled=True)  5.18 us
    dot_general x1, matrix products, shards(): jnp.einsum('psd,fd->psf', incoming, up_block, preferred_element_type=jnp....  2.54 us
    dot_general x1, matrix products, shards(): jnp.dot(active, down_block, preferred_element_type=jnp.float32)  2.38 us
  transfers between devices with their start and end apart: 2, of which 2 were waited for; matrix products, arithmetic and copies ran while one was open for 0% of the time, Pallas kernels for 0%

commit v1 on v0

--- a/solution.py
+++ b/solution.py
@@ -6,6 +6,12 @@
 EXPERTS = 8
 CAP = 7
 SLOTS = 8
+
+
+def exchange_blocks(value, axis, split, join):
+    pieces = jnp.split(value, lax.axis_size(axis), axis=split)
+    received = lax.all_to_all(jnp.stack(pieces), axis, 0, 0)
+    return jnp.concatenate(received, axis=join)
 
 
 def passed_along(shard, axis, by):
@@ -47,7 +53,7 @@
     picker = jnp.any(hits, axis=2).astype(jnp.bfloat16)
     outgoing = jnp.dot(picker, normed, preferred_element_type=jnp.float32).astype(jnp.bfloat16)
     outgoing = outgoing.reshape(SLOTS, members, width)
-    incoming = lax.all_to_all(outgoing, "expert", split_axis=1, concat_axis=1, tiled=True)
+    incoming = exchange_blocks(outgoing, "expert", 1, 1)
     inner = jnp.einsum("psd,fd->psf", incoming, up_block, preferred_element_type=jnp.float32)
     active = jax.nn.silu(inner).astype(jnp.bfloat16)
     active = lax.optimization_barrier(active.transpose(1, 0, 2).reshape(members * SLOTS, -1))

time: 109 us -> 113 us (1.037)
  local copies, waits for them, and re-layouts: 2.05 us -> 5.73 us
    split x0 -> x1, local copies, waits for them, and re-layouts: none -> 4.03 us  [exchange_blocks(): pieces = jnp.split(value, lax.axis_size(axis), axis=split)]
where the time goes in v1:
time: 113 us
  blocking collectives  48.2 us (43%)
  waiting for transfers between devices  43.3 us (38%)
  starting transfers between devices  6.71 us (6%)
  matrix products  6.53 us (6%)
  local copies, waits for them, and re-layouts  5.73 us (5%)
  other arithmetic  2.12 us (2%)
    all_to_all x1, blocking collectives, exchange_blocks(): received = lax.all_to_all(jnp.stack(pieces), axis, 0, 0)  48.2 us
    all_to_all x1, waiting for transfers between devices, shards(): lax.all_to_all(partial, 'expert', split_axis=0, concat_axis=0, tiled=True)  42.2 us
    all_to_all x1, starting transfers between devices, shards(): lax.all_to_all(partial, 'expert', split_axis=0, concat_axis=0, tiled=True)  5.18 us
    split x1, local copies, waits for them, and re-layouts, exchange_blocks(): pieces = jnp.split(value, lax.axis_size(axis), axis=split)  4.03 us
    dot_general x1, matrix products, shards(): jnp.einsum('psd,fd->psf', incoming, up_block, preferred_element_type=jnp....  2.55 us
    dot_general x1, matrix products, shards(): jnp.dot(active, down_block, preferred_element_type=jnp.float32)  2.4 us
  transfers between devices with their start and end apart: 2, of which 2 were waited for; matrix products, arithmetic and copies ran while one was open for 0% of the time, Pallas kernels for 0%

profile of v1, /device:TPU:13, one launch (start us, length us, event | category | flops | bytes accessed | tf_op | source)
XLA Modules:
  0.0 112.8 jit_solution(6267057299949990083)
XLA Ops:
  0.0 0.7 fusion.43
  0.7 1.0 maximum_convert_fusion
  1.7 0.2 multiply_reduce_fusion
  1.9 0.1 convolution_add_fusion
  2.0 0.1 multiply_reduce_fusion.1
  2.1 0.1 compare_reduce_fusion
  2.2 0.7 convolution_convert_fusion.1
  2.8 0.0 slice-start
  2.9 4.0 %fusion.45 = (bf16[8,1,7168]{2,1,0:T(2,128)(2,1)S(1)}, bf16[8,1,7168]{2,1,0:T(2,128)(2,1)S(1)}, bf16[8,1,7168]{2,1,0:T(2,128)(2,1)S(1)}, bf16[8,1,7168]{2,1,0:T(...) fusion(bf16[8,16,7168]{2,1,0:T(8,128)(2,1)S(1)} %bitcast.132), kind=kLoop, calls=%fused_computation.75 | loop fusion | bytes 3670016 | tf_op jit(solution)/shard_map/split | solution.py:12
  7.0 0.0 slice-start.1
  7.7 48.2 %all_to_all.10 = bf16[16,8,1,7168]{3,1,2,0:T(8,128)(2,1)S(1)} all-to-all(bf16[16,8,1,7168]{3,1,2,0:T(8,128)(2,1)S(1)} %fusion.26), channel_id=1, replica_groups=mesh['segment'=2,'expert'=16] {'expert'}, dimensions={0} | all-to-all | bytes 3670016 | tf_op jit(solution)/shard_map/all_to_all | solution.py:13
  55.9 2.5 %fusion.19 = bf16[128,512]{1,0:T(8,128)(2,1)S(1)} fusion(bf16[1,512,7168]{2,1,0:T(8,128)(2,1)S(1)} %bitcast.129, bf16[16,8,1,7168]{3,1,2,0:T(8,128)(2,1)S(1)} %all_to_all.10), kind=kOutput, calls=%fused_computation.20 | convolution fusion | flops 939851776 | bytes 9306112 | tf_op jit(solution)/shard_map/psd,fd->psf/dot_general | solution.py:57
  58.5 2.4 %fusion = bf16[16,8,7168]{2,1,0:T(8,128)(2,1)} fusion(bf16[128,512]{1,0:T(8,128)(2,1)S(1)} %fusion.19, bf16[1,512,7168]{2,1,0:T(8,128)(2,1)S(1)} %bitcast.131), kind=kOutput, calls=%fused_computation.2 | convolution fusion | flops 940441600 | bytes 9306112 | tf_op jit(solution)/shard_map/dot_general | solution.py:60
  60.9 5.2 %all-to-all-start.1 = ((bf16[16,8,7168]{2,1,0:T(8,128)(2,1)}), bf16[16,8,7168]{2,1,0:T(8,128)(2,1)S(1)}, u32[]{:S(2)}, u32[]{:S(2)}) async-start(bf16[16,8,7168]{2,1,0:T(8,128)(2,1)} %fusion), calls=%async_computation.1 | async-start | bytes 3670016 | tf_op jit(solution)/shard_map/all_to_all | solution.py:62
  66.1 0.1 fusion.42
  66.1 0.1 reshape.74
  66.2 0.1 copy.127
  66.4 0.1 copy.126
  66.5 42.2 %all-to-all-done.1 = bf16[16,8,7168]{2,1,0:T(8,128)(2,1)S(1)} async-done(((bf16[16,8,7168]{2,1,0:T(8,128)(2,1)}), bf16[16,8,7168]{2,1,0:T(8,128)(2,1)S(1)}, u32[]{:S(2)}, u32[]{:S(2)}) %all-to-all-start.1) | async-done | bytes 1835040 | tf_op jit(solution)/shard_map/all_to_all | solution.py:62
  108.7 0.4 convolution_bitcast_fusion
  109.1 0.4 fusion.3
  109.5 1.5 %collective-permute-start = (bf16[16,7168]{1,0:T(8,128)(2,1)S(1)}, bf16[16,7168]{1,0:T(8,128)(2,1)S(1)}, u32[]{:S(2)}, u32[]{:S(2)}) collective-permute-start(bf16[16,7168]{1,0:T(8,128)(2,1)S(1)} %fusion.3), channel_id=1, source_target_pairs={{0,16},{16,0},{1,17},{17,1},{2,18},{18,2},{3,19},{19,3},{4,20},{20... | collective-permute-start | bytes 688136 | tf_op jit(solution)/shard_map/ppermute | solution.py:19
  111.0 1.1 collective-permute-done
  112.1 0.7 copy.208
  (34 shorter events, 0.7 us)
Async XLA Ops:
  2.8 53.0 %slice-start = ((s8[7340032]{0:T(1024)(128)(4,1)}), s8[4194304]{0:T(1024)(128)(4,1)S(1)}, s32[]{:S(2)}) async-start(s8[7340032]{0:T(1024)(128)(4,1)} %bitcast.128), calls=%async_computation.2 | async-start | bytes 8388608
  7.0 48.9 %slice-start.1 = ((s8[7340032]{0:T(1024)(128)(4,1)}), s8[3145728]{0:T(1024)(128)(4,1)S(1)}, s32[]{:S(2)}) async-start(s8[7340032]{0:T(1024)(128)(4,1)} %bitcast.128), calls=%async_computation.3 | async-start | bytes 6291456
  7.7 50.7 %slice-start.2 = ((s8[7340032]{0:T(1024)(128)(4,1)}), s8[4194304]{0:T(1024)(128)(4,1)S(1)}, s32[]{:S(2)}) async-start(s8[7340032]{0:T(1024)(128)(4,1)} %bitcast.130), calls=%async_computation.4 | async-start | bytes 8388608
  55.9 2.6 %slice-start.3 = ((s8[7340032]{0:T(1024)(128)(4,1)}), s8[3145728]{0:T(1024)(128)(4,1)S(1)}, s32[]{:S(2)}) async-start(s8[7340032]{0:T(1024)(128)(4,1)} %bitcast.130), calls=%async_computation.5 | async-start | bytes 6291456
  60.9 5.2 %copy-start.1 = (f32[1,16,2]{1,2,0:T(2,128)S(1)}, f32[1,16,2]{1,2,0:T(2,128)}, u32[]{:S(2)}) copy-start(f32[1,16,2]{1,2,0:T(2,128)} %param.11) | copy-start | bytes 388
  60.9 47.8 %all-to-all-start.1 = ((bf16[16,8,7168]{2,1,0:T(8,128)(2,1)}), bf16[16,8,7168]{2,1,0:T(8,128)(2,1)S(1)}, u32[]{:S(2)}, u32[]{:S(2)}) async-start(bf16[16,8,7168]{2,1,0:T(8,128)(2,1)} %fusion), calls=%async_computation.1 | async-start | bytes 3670016 | tf_op jit(solution)/shard_map/all_to_all | solution.py:62
  66.0 43.0 %copy-start = (bf16[1,16,7168]{2,1,0:T(8,128)(2,1)S(1)}, bf16[1,16,7168]{2,1,0:T(8,128)(2,1)}, u32[]{:S(2)}) copy-start(bf16[1,16,7168]{2,1,0:T(8,128)(2,1)} %param.6) | copy-start | bytes 688132
  109.5 2.6 %collective-permute-start = (bf16[16,7168]{1,0:T(8,128)(2,1)S(1)}, bf16[16,7168]{1,0:T(8,128)(2,1)S(1)}, u32[]{:S(2)}, u32[]{:S(2)}) collective-permute-start(bf16[16,7168]{1,0:T(8,128)(2,1)S(1)} %fusion.3), channel_id=1, source_target_pairs={{0,16},{16,0},{1,17},{17,1},{2,18},{18,2},{3,19},{19,3},{4,20},{20... | collective-permute-start | bytes 688136 | tf_op jit(solution)/shard_map/ppermute | solution.py:19
